TPU v7x, 128 devices: a whole 4x4x4 slice. The times are simulated.
128 devices in a mesh: node: 4 (over x), ep: 32 (over y, z, core).
Axes of the slice: x: 4, y: 4, z: 4, core: 2. Of those that a mesh axis runs over, the one named last changes fastest.
Arguments:
- images: bfloat16 [128, 257, 1280], P(('node', 'ep')), may hold values from -6 to 6
- w_query: bfloat16 [1280, 1280], P(None, 'node'), may hold values from -6 to 6
- w_key: bfloat16 [1280, 1280], P(None, 'node'), may hold values from -6 to 6
- w_value: bfloat16 [1280, 1280], P(None, 'node'), may hold values from -0.15625 to 0.15625
- w_output: bfloat16 [1280, 1280], replicated, may hold values from -0.15625 to 0.15625
- router: bfloat16 [1280, 32], replicated, may hold values from -0.15625 to 0.15625
- w_in: bfloat16 [32, 1280, 5120], P('ep', None, 'node'), may hold values from -0.15625 to 0.15625
- w_out: bfloat16 [32, 5120, 1280], P('ep', 'node'), may hold values from -0.078125 to 0.078125
- routes: int32 [128, 257, 2], P(('node', 'ep')), may hold values from 0 to 31, all different within a row; in each aligned block of 257 rows (0 to 256, 257 to 513, ..., all dimensions but the last counted through in order) at most 24 rows name the same one
Outputs:
- output: bfloat16 [128, 257, 1280], P(('node', 'ep'))
Inputs may be any that keep to these rules, and one draw needn't show every extreme that they name: `routes`: the two experts of a token differ. At most 24 tokens of one image name the same expert, and in every draw some image has an expert named by exactly 24 of its tokens.
All inputs are finite; a program needn't handle non-finite values.
Results may differ from a plain program's by a relative error of at most 0.0085.
Values may be sent and summed in bfloat16 or wider, within the bound.
No kernel may reach another device: no remote copies, remote signals or barrier semaphores. Data moves between devices by JAX's collectives and lax.ppermute only.
A program may use at most 128 MiB of HBM per device.

v0:
```python
import math
import jax
import jax.numpy as jnp
from jax import lax
from jax.sharding import PartitionSpec as P

D = 1280
HEADS = 16
CAP = 24


def layer_norm(values):
    center = values - jnp.mean(values, axis=-1, keepdims=True)
    spread = jnp.mean(center * center, axis=-1, keepdims=True)
    return center * lax.rsqrt(spread + 1e-06)


def slot_table(chosen, num_experts):
    onehot = (chosen[..., None] == jnp.arange(num_experts, dtype=jnp.int32)).astype(jnp.int32)
    before = jnp.cumsum(onehot, axis=1) - onehot
    return jnp.sum(before * onehot, axis=-1)


def shards(images, w_query, w_key, w_value, w_output, router, w_in, w_out, routes):
    local_images, tokens_dev, width = images.shape
    head_size = D // HEADS
    local_heads = w_query.shape[1] // head_size
    node_count = lax.axis_size("node")
    column_count = lax.axis_size("ep")
    num_experts = router.shape[1]
    local_experts = w_in.shape[0]
    slot_count = local_images * CAP
    inputs = images.astype(jnp.float32)
    normed = layer_norm(inputs).astype(jnp.bfloat16)
    shard_rows = lax.all_gather(normed, "node", axis=0, tiled=True)
    number = shard_rows.shape[0]
    queries = jnp.einsum(
        "ctd,de->cte", shard_rows, w_query, preferred_element_type=jnp.float32
    ).astype(jnp.bfloat16)
    projected_keys = jnp.einsum(
        "ctd,de->cte", shard_rows, w_key, preferred_element_type=jnp.float32
    ).astype(jnp.bfloat16)
    projected_values = jnp.einsum(
        "ctd,de->cte", shard_rows, w_value, preferred_element_type=jnp.float32
    ).astype(jnp.bfloat16)
    query_heads = queries.reshape(number, tokens_dev, local_heads, head_size)
    key_heads = projected_keys.reshape(number, tokens_dev, local_heads, head_size)
    value_heads = projected_values.reshape(number, tokens_dev, local_heads, head_size)
    scores = jnp.einsum(
        "cqhd,ckhd->chqk", query_heads, key_heads, preferred_element_type=jnp.float32
    ) / math.sqrt(head_size)
    weights = jax.nn.softmax(scores, axis=-1).astype(jnp.bfloat16)
    mixture = jnp.einsum(
        "chqk,ckhd->cqhd", weights, value_heads, preferred_element_type=jnp.float32
    ).astype(jnp.bfloat16)
    head_results = mixture.reshape(number, tokens_dev, local_heads * head_size)
    attention = jnp.einsum(
        "itd,de->ite",
        lax.all_to_all(head_results, "node", split_axis=0, concat_axis=2, tiled=True),
        w_output,
        preferred_element_type=jnp.float32,
    )
    middle = inputs + attention
    normed_second = layer_norm(middle).astype(jnp.bfloat16)
    logits = jnp.einsum("itd,de->ite", normed_second, router, preferred_element_type=jnp.float32)
    chosen_mask = routes[..., None] == jnp.arange(num_experts, dtype=jnp.int32)
    chosen_logit = jnp.sum(jnp.where(chosen_mask, logits[:, :, None, :], jnp.float32(0.0)), axis=-1)
    gate_values = jax.nn.sigmoid(chosen_logit)
    flat_routes = routes.reshape(local_images, 2 * tokens_dev)
    slot_index = slot_table(flat_routes, num_experts)
    image_base = jnp.arange(local_images, dtype=jnp.int32)[:, None] * CAP
    position = (flat_routes * slot_count + image_base + slot_index).reshape(-1)
    token_ids = jnp.arange(local_images * 2 * tokens_dev, dtype=jnp.int32) // 2
    source = jnp.full((num_experts * slot_count,), -1, jnp.int32).at[position].set(token_ids)
    token_rows = normed_second.reshape(local_images * tokens_dev, width)
    gathered = jnp.take(token_rows, jnp.maximum(source, 0), axis=0)
    gathered = jnp.where(source[:, None] >= 0, gathered, jnp.zeros_like(gathered))
    outgoing = gathered.reshape(column_count, local_experts, slot_count, width)
    copies = jnp.broadcast_to(outgoing[None], (node_count,) + outgoing.shape)
    copies = copies.reshape(node_count * column_count, local_experts, slot_count, width)
    arrived = lax.all_to_all(copies, ("node", "ep"), split_axis=0, concat_axis=0, tiled=True)
    pre_act = jnp.einsum("lesd,edf->lesf", arrived, w_in, preferred_element_type=jnp.float32)
    hidden = jax.nn.gelu(pre_act, approximate=True).astype(jnp.bfloat16)
    partial_sum = jnp.einsum(
        "lesf,efd->lesd", hidden, w_out, preferred_element_type=jnp.float32
    ).astype(jnp.bfloat16)
    returned = lax.all_to_all(partial_sum, ("node", "ep"), split_axis=0, concat_axis=0, tiled=True)
    returned = returned.astype(jnp.float32).reshape(
        node_count, column_count, local_experts, slot_count, width
    )
    expert_result = jnp.sum(returned, axis=0).astype(jnp.bfloat16)
    result_rows = expert_result.reshape(num_experts * slot_count, width)
    picked = jnp.take(result_rows, position, axis=0).reshape(local_images, tokens_dev, 2, width)
    expert_mix = jnp.sum(gate_values[..., None] * picked.astype(jnp.float32), axis=2)
    return (middle + expert_mix).astype(jnp.bfloat16)


def solution(mesh):
    placed = (
        P(("node", "ep"), None, None),
        P(None, "node"),
        P(None, "node"),
        P(None, "node"),
        P(),
        P(),
        P("ep", None, "node"),
        P("ep", "node", None),
        P(("node", "ep"), None, None),
    )
    return jax.shard_map(
        shards, mesh=mesh, in_specs=placed, out_specs=P(("node", "ep"), None, None), check_vma=False
    )
```

profile of v0, /device:TPU:97, one launch (start us, length us, event | category | flops | bytes accessed | tf_op | source)
XLA Modules:
  0.0 396.5 jit_solution(17544285698891339135)
XLA Ops:
  6.5 1.4 convert_reduce_fusion
  8.0 1.4 fusion.34
  9.4 2.3 fusion.35
  12.4 1.5 reduce-window.6
  15.9 4.1 %scatter_custom_fusion = s32[768]{0:T(1024)S(1)} fusion(s32[514]{0:T(1024)S(1)} %fusion.49, s32[514]{0:T(1024)S(1)} %add_select_fusion, s32[]{:T(128)} %constant.77.clone.1), kind=kCustom, calls=%fused_computation.80 | custom fusion | bytes 3076 | tf_op jit(solution)/shard_map/scatter | solution.py:74
  20.0 28.8 %all-gather.2.cloned.1.call-done = bf16[4,257,1280]{2,1,0:T(8,128)(2,1)} async-done(((bf16[1,257,1280]{2,1,0:T(8,128)(2,1)}), bf16[4,257,1280]{2,1,0:T(8,128)(2,1)}) %all-gather.2.cloned.1.call-update) | async-done | bytes 2631696 | tf_op jit(solution)/shard_map/all_gather | solution.py:35
  48.8 4.4 %convolution_convert_fusion = bf16[4,257,320]{2,1,0:T(8,128)(2,1)} fusion(bf16[4,257,1280]{2,1,0:T(8,128)(2,1)} %all-gather.2.cloned.1.call-done, bf16[1280,320]{0,1:T(8,128)(2,1)} %param.11), kind=kOutput, calls=%fused_computation.37 | convolution fusion | flops 842466560 | bytes 4108800 | tf_op jit(solution)/shard_map/ctd,de->cte/dot_general | solution.py:40
  53.2 2.3 copy.95
  55.5 4.4 %convolution_convert_fusion.2 = bf16[4,257,320]{2,1,0:T(8,128)(2,1)} fusion(bf16[4,257,1280]{2,1,0:T(8,128)(2,1)} %all-gather.2.cloned.1.call-done, bf16[1280,320]{0,1:T(8,128)(2,1)} %param.12), kind=kOutput, calls=%fused_computation.39 | convolution fusion | flops 842466560 | bytes 4108800 | tf_op jit(solution)/shard_map/ctd,de->cte/dot_general | solution.py:43
  59.9 2.2 copy.93
  62.2 4.4 %convolution_convert_fusion.1 = bf16[4,257,320]{2,1,0:T(8,128)(2,1)} fusion(bf16[4,257,1280]{2,1,0:T(8,128)(2,1)} %all-gather.2.cloned.1.call-done, bf16[1280,320]{0,1:T(8,128)(2,1)} %param.10), kind=kOutput, calls=%fused_computation.38 | convolution fusion | flops 842466560 | bytes 4108800 | tf_op jit(solution)/shard_map/ctd,de->cte/dot_general | solution.py:37
  66.6 2.3 copy.94
  68.9 6.5 %fusion.57 = (f32[4,4,257]{2,1,0:T(4,128)S(1)}, f32[4,4,257,257]{2,3,1,0:T(8,128)}) fusion(bf16[4,257,4,80]{1,3,2,0:T(8,128)(2,1)} %bitcast.114, bf16[4,257,4,80]{1,3,2,0:T(8,128)(2,1)} %bitcast.113), kind=kOutput, calls=%fused_computation.92 | convolution fusion | flops 172256048 | bytes 5559424 | tf_op jit(solution)/shard_map/sub | solution.py:52
  75.4 5.1 %fusion.33 = bf16[4,4,80,257]{3,2,1,0:T(8,128)(2,1)} fusion(bf16[4,257,4,80]{1,3,2,0:T(8,128)(2,1)} %bitcast.112, f32[4,4,257,257]{2,3,1,0:T(8,128)} %get-tuple-element.8, f32[4,4,257]{2,1,0:T(4,128)S(1)} %get-tuple-element.7), kind=kOutput, calls=%fused_computation.36 | convolution fusion | flops 171527968 | bytes 5559424 | tf_op jit(solution)/shard_map/chqk,ckhd->cqhd/dot_general | solution.py:53
  80.5 2.2 copy.97
  82.8 4.4 %all-to-all-start = ((bf16[4,257,320]{2,1,0:T(8,128)(2,1)}), bf16[4,257,320]{2,1,0:T(8,128)(2,1)}, u32[]{:S(2)}, u32[]{:S(2)}) async-start(bf16[4,257,320]{2,1,0:T(8,128)(2,1)} %copy.97), calls=%async_computation | async-start | bytes 1622016 | tf_op jit(solution)/shard_map/all_to_all | solution.py:59
  87.4 11.5 %all-to-all-done = bf16[4,257,320]{2,1,0:T(8,128)(2,1)} async-done(((bf16[4,257,320]{2,1,0:T(8,128)(2,1)}), bf16[4,257,320]{2,1,0:T(8,128)(2,1)}, u32[]{:S(2)}, u32[]{:S(2)}) %all-to-all-start) | async-done | bytes 657952 | tf_op jit(solution)/shard_map/all_to_all | solution.py:59
  98.8 2.3 copy.98
  101.2 2.5 reshape.358
  103.7 3.4 fusion.58
  108.3 1.1 fusion.40
  109.3 6.4 %gather_fusion = bf16[768,1280]{1,0:T(8,128)(2,1)} fusion(bf16[257,1280]{1,0:T(8,128)(2,1)} %fusion.40, s32[1024]{0:T(1024)S(1)} %pad_clamp_fusion.1), kind=kCustom, calls=%fused_computation | custom fusion | bytes 3935232 | tf_op jit(solution)/shard_map/jit(_take)/gather | solution.py:76
  115.7 1.9 select_select_fusion
  118.1 99.0 %all_to_all.25 = bf16[128,1,24,1280]{3,2,1,0:T(8,128)(2,1)} all-to-all(bf16[128,1,24,1280]{3,2,1,0:T(8,128)(2,1)S(1)} %bitcast.110), channel_id=1, replica_groups=mesh['node'=4,'ep'=32] {'node','ep'}, dimensions={0} | all-to-all | bytes 15728640 | tf_op jit(solution)/shard_map/all_to_all | solution.py:81
  217.1 25.9 %convert_bitcast_fusion = bf16[128,1,24,1280]{3,0,2,1:T(8,128)(2,1)} fusion(bf16[1,1280,1280]{2,1,0:T(8,128)(2,1)S(1)} %copy-done, bf16[128,1,24,1280]{3,2,1,0:T(8,128)(2,1)} %all_to_all.25, bf16[1,1280,1280]{2,1,0:T(8,128)(2,1)} %param.15), kind=kOutput, calls=%fused_computation.18 | convolution fusion | flops 20171980800 | bytes 22282240 | tf_op jit(solution)/shard_map/lesf,efd->lesd/dot_general | solution.py:84
  243.0 10.8 %copy.108 = bf16[128,1,24,1280]{3,2,1,0:T(8,128)(2,1)} copy(bf16[128,1,24,1280]{3,0,2,1:T(8,128)(2,1)} %convert_bitcast_fusion) | data formatting | bytes 15728640 | tf_op jit(solution)/shard_map/convert_element_type | solution.py:86
  253.8 10.7 %all-to-all-start.2 = ((bf16[128,1,24,1280]{3,2,1,0:T(8,128)(2,1)}), bf16[128,1,24,1280]{3,2,1,0:T(8,128)(2,1)}, u32[]{:S(2)}, u32[]{:S(2)}) async-start(bf16[128,1,24,1280]{3,2,1,0:T(8,128)(2,1)} %copy.108), calls=%async_computation.2 | async-start | bytes 15728640 | tf_op jit(solution)/shard_map/all_to_all | solution.py:87
  265.5 97.6 %all-to-all-done.2 = bf16[128,1,24,1280]{3,2,1,0:T(8,128)(2,1)} async-done(((bf16[128,1,24,1280]{3,2,1,0:T(8,128)(2,1)}), bf16[128,1,24,1280]{3,2,1,0:T(8,128)(2,1)}, u32[]{:S(2)}, u32[]{:S(2)}) %all-to-all-start.2) | async-done | bytes 7864352 | tf_op jit(solution)/shard_map/all_to_all | solution.py:87
  363.1 4.3 %bitcast_reduce_fusion = bf16[32,24,1280]{2,1,0:T(8,128)(2,1)S(1)} fusion(bf16[4,32,24,1280]{3,2,1,0:T(8,128)(2,1)} %bitcast.107), kind=kLoop, calls=%fused_computation.13 | loop fusion | flops 2949120 | bytes 9830400 | tf_op jit(solution)/shard_map/reduce_sum | solution.py:91
  367.4 3.5 gather_fusion.1
  370.9 4.1 %gather.15 = bf16[1,257,2,1280]{3,2,1,0:T(2,128)(2,1)} reshape(bf16[514,1280]{1,0:T(8,128)(2,1)} %gather_fusion.1) | data formatting | bytes 2631680 | tf_op jit(solution)/shard_map/jit(_take)/gather | solution.py:93
  375.0 13.6 %multiply_reduce_fusion.1 = f32[257,1280]{1,0:T(8,128)S(1)} fusion(bf16[1,257,2,1280]{3,2,1,0:T(2,128)(2,1)} %gather.15, pred[257,2]{1,0:T(8,128)(4,1)S(1)} %copy.105, f32[257,2]{1,0:T(8,128)S(1)} %copy.99), kind=kLoop, calls=%fused_computation.29 | loop fusion | flops 2302720 | bytes 2634250 | tf_op jit(solution)/shard_map/reduce_sum | solution.py:94
  (55 shorter events, 6.4 us)
Async XLA Ops:
  6.5 210.6 %copy-start = (bf16[1,1280,1280]{2,1,0:T(8,128)(2,1)S(1)}, bf16[1,1280,1280]{2,1,0:T(8,128)(2,1)}, u32[]{:S(2)}) copy-start(bf16[1,1280,1280]{2,1,0:T(8,128)(2,1)} %param.16) | copy-start | bytes 9830404
  6.5 5.2 %copy-start.6 = (s32[1,257,2]{1,2,0:T(2,128)S(1)}, s32[1,257,2]{1,2,0:T(2,128)}, u32[]{:S(2)}) copy-start(s32[1,257,2]{1,2,0:T(2,128)} %param.17) | copy-start | bytes 6172
  6.5 42.2 %all-gather.2.cloned.1.call-start = ((), (), s32[]{:S(2)}) async-start(), calls=%async_computation.3 | async-start | bytes 3379200 | tf_op jit(solution)/shard_map/all_gather | solution.py:35
  82.8 16.1 %all-to-all-start = ((bf16[4,257,320]{2,1,0:T(8,128)(2,1)}), bf16[4,257,320]{2,1,0:T(8,128)(2,1)}, u32[]{:S(2)}, u32[]{:S(2)}) async-start(bf16[4,257,320]{2,1,0:T(8,128)(2,1)} %copy.97), calls=%async_computation | async-start | bytes 1622016 | tf_op jit(solution)/shard_map/all_to_all | solution.py:59
  107.2 1.1 copy-start.3
  253.8 11.2 %copy-start.2 = (bf16[257,1280]{1,0:T(8,128)(2,1)S(1)}, bf16[257,1280]{1,0:T(8,128)(2,1)}, u32[]{:S(2)}) copy-start(bf16[257,1280]{1,0:T(8,128)(2,1)} %fusion.40) | copy-start | bytes 1973764
  253.8 11.2 %copy-start.5 = (bf16[1280,32]{0,1:T(8,128)(2,1)S(1)}, bf16[1280,32]{0,1:T(8,128)(2,1)}, u32[]{:S(2)}) copy-start(bf16[1280,32]{0,1:T(8,128)(2,1)} %param.14) | copy-start | bytes 245764
  253.8 109.4 %all-to-all-start.2 = ((bf16[128,1,24,1280]{3,2,1,0:T(8,128)(2,1)}), bf16[128,1,24,1280]{3,2,1,0:T(8,128)(2,1)}, u32[]{:S(2)}, u32[]{:S(2)}) async-start(bf16[128,1,24,1280]{3,2,1,0:T(8,128)(2,1)} %copy.108), calls=%async_computation.2 | async-start | bytes 15728640 | tf_op jit(solution)/shard_map/all_to_all | solution.py:87
  370.9 18.7 %copy-start.1 = (bf16[1,1280,1280]{2,1,0:T(8,128)(2,1)S(1)}, bf16[1,1280,1280]{2,1,0:T(8,128)(2,1)}, u32[]{:S(2)}) copy-start(bf16[1,1280,1280]{2,1,0:T(8,128)(2,1)} %param.16) | copy-start | bytes 9830404
  375.0 13.6 %copy-start.4 = (f32[1,257,1280]{2,1,0:T(8,128)S(1)}, f32[1,257,1280]{2,1,0:T(8,128)}, u32[]{:S(2)}) copy-start(f32[1,257,1280]{2,1,0:T(8,128)} %copy-done.3) | copy-start | bytes 3947524
Sparse Core Ops, SparseCore 0:
  11.8 36.8 all-gather.1
where the time goes:
time: 397 us; the launch traced here: 396 us
  waiting for transfers between devices  138 us (35%)
  blocking collectives  99 us (25%)
  matrix products  54.6 us (14%)
  local copies, waits for them, and re-layouts  46.4 us (12%)
  other arithmetic  29.8 us (8%)
  starting transfers between devices  15.1 us (4%)
  between operations  13.7 us (3%)
    all_to_all x1, blocking collectives, shards(): lax.all_to_all(copies, ('node', 'ep'), split_axis=0, concat_axis=0, tiled...  99 us
    all_to_all x1, waiting for transfers between devices, shards(): lax.all_to_all(partial_sum, ('node', 'ep'), split_axis=0, concat_axis=0,...  97.6 us
    all_gather x1, waiting for transfers between devices, shards(): shard_rows = lax.all_gather(normed, 'node', axis=0, tiled=True)  28.8 us
    dot_general x1, matrix products, shards(): jnp.einsum('lesf,efd->lesd', hidden, w_out, preferred_element_type=jnp.fl...  25.9 us
    reduce_sum x1, other arithmetic, shards(): jnp.sum(gate_values[..., None] * picked.astype(jnp.float32), axis=2)  13.6 us
    all_to_all x1, waiting for transfers between devices, shards(): lax.all_to_all(head_results, 'node', split_axis=0, concat_axis=2, tiled=T...  11.5 us
    convert_element_type x1, local copies, waits for them, and re-layouts, shards(): partial_sum = jnp.einsum('lesf,efd->lesd', hidden, w_out, preferred_eleme...  10.8 us
    all_to_all x1, starting transfers between devices, shards(): lax.all_to_all(partial_sum, ('node', 'ep'), split_axis=0, concat_axis=0,...  10.7 us
  transfers between devices with their start and end apart: 3, of which 3 were waited for; matrix products, arithmetic and copies ran while one was open for 2% of the time, Pallas kernels for 0%

commit v1 on v0

--- a/solution.py
+++ b/solution.py
@@ -32,7 +32,19 @@
     slot_count = local_images * CAP
     inputs = images.astype(jnp.float32)
     normed = layer_norm(inputs).astype(jnp.bfloat16)
-    shard_rows = lax.all_gather(normed, "node", axis=0, tiled=True)
+    n_parts = jax.lax.axis_size("node")
+    in_order = [(dev_i, (dev_i + 1) % n_parts) for dev_i in range(n_parts)]
+    crops = [(dev_i, (dev_i - 1) % n_parts) for dev_i in range(n_parts)]
+    z_new, known = ([normed], [normed])
+    for _ in range(n_parts // 2):
+        small = jax.lax.ppermute(z_new[-1], "node", in_order)
+        z_new.append(small)
+    at = 0
+    while at < (n_parts - 1) // 2:
+        known.append(jax.lax.ppermute(known[-1], "node", crops))
+        at += 1
+    m_next = jnp.concatenate([*z_new[::-1], *known[1:]], 0)
+    shard_rows = jnp.roll(m_next, (jax.lax.axis_index("node") - n_parts // 2) * normed.shape[0], 0)
     number = shard_rows.shape[0]
     queries = jnp.einsum(
         "ctd,de->cte", shard_rows, w_query, preferred_element_type=jnp.float32

time: 397 us -> 395 us (level)
  between operations: 13.7 us -> 0.63 us
  local copies, waits for them, and re-layouts: 46.4 us -> 56.7 us
  waiting for transfers between devices: 138 us -> 132 us
    all_gather x1 -> x0, waiting for transfers between devices: 28.8 us -> none  [shards(): shard_rows = lax.all_gather(normed, 'node', axis=0, tiled=True)]
    ppermute x0 -> x3, waiting for transfers between devices: none -> 24.5 us  [the longest x2 24.5 us: shards(): small = jax.lax.ppermute(z_new[-1], 'node', in_order)]
    unnamed x15 -> x30, local copies, waits for them, and re-layouts: 0.91 us -> 9.78 us
  transfers between devices with their start and end apart: 3 -> 5, of which waited for: 3 -> 4; matrix products, arithmetic and copies ran while one was open for 2% -> 4% of each run, Pallas kernels for 0% -> 0%
where the time goes in v1:
time: 395 us; the launch traced here: 391 us
  waiting for transfers between devices  132 us (33%)
  blocking collectives  102 us (26%)
  local copies, waits for them, and re-layouts  56.7 us (14%)
  matrix products  50.9 us (13%)
  other arithmetic  31.5 us (8%)
  starting transfers between devices  17.2 us (4%)
    all_to_all x1, blocking collectives, shards(): lax.all_to_all(copies, ('node', 'ep'), split_axis=0, concat_axis=0, tiled...  102 us
    all_to_all x1, waiting for transfers between devices, shards(): lax.all_to_all(partial_sum, ('node', 'ep'), split_axis=0, concat_axis=0,...  98.2 us
    dot_general x1, matrix products, shards(): jnp.einsum('lesf,efd->lesd', hidden, w_out, preferred_element_type=jnp.fl...  25.9 us
    ppermute x2, waiting for transfers between devices, shards(): small = jax.lax.ppermute(z_new[-1], 'node', in_order)  24.5 us
    reduce_sum x1, other arithmetic, shards(): jnp.sum(gate_values[..., None] * picked.astype(jnp.float32), axis=2)  13.6 us
    convert_element_type x1, local copies, waits for them, and re-layouts, shards(): partial_sum = jnp.einsum('lesf,efd->lesd', hidden, w_out, preferred_eleme...  10.8 us
    all_to_all x1, starting transfers between devices, shards(): lax.all_to_all(partial_sum, ('node', 'ep'), split_axis=0, concat_axis=0,...  9.98 us
    unnamed x30, local copies, waits for them, and re-layouts  9.78 us
  transfers between devices with their start and end apart: 5, of which 4 were waited for; matrix products, arithmetic and copies ran while one was open for 4% of the time, Pallas kernels for 0%

profile of v1, /device:TPU:97, one launch (start us, length us, event | category | flops | bytes accessed | tf_op | source)
XLA Modules:
  0.0 391.0 jit_solution(6780929691269503147)
XLA Ops:
  2.9 2.3 fusion.50
  5.2 2.5 collective-permute-start.2
  8.6 1.5 reduce-window.6
  10.4 14.6 %collective-permute-done = bf16[1,257,1280]{2,1,0:T(8,128)(2,1)} collective-permute-done((bf16[1,257,1280]{2,1,0:T(8,128)(2,1)}, bf16[1,257,1280]{2,1,0:T(8,128)(2,1)}, u32[]{:S(2)}, u32[]{:S(2)}) %collective-permute-start) | collective-permute-done | bytes 657952 | tf_op jit(solution)/shard_map/ppermute | solution.py:40
  27.1 4.4 %scatter_custom_fusion = s32[768]{0:T(1024)S(1)} fusion(s32[514]{0:T(1024)S(1)} %fusion.64, s32[514]{0:T(1024)S(1)} %add_select_fusion, s32[]{:T(128)} %constant.106.clone.1), kind=kCustom, calls=%fused_computation.94 | custom fusion | bytes 3076 | tf_op jit(solution)/shard_map/scatter | solution.py:86
  31.5 9.9 %collective-permute-done.1 = bf16[1,257,1280]{2,1,0:T(8,128)(2,1)} collective-permute-done((bf16[1,257,1280]{2,1,0:T(8,128)(2,1)}, bf16[1,257,1280]{2,1,0:T(8,128)(2,1)}, u32[]{:S(2)}, u32[]{:S(2)}) %collective-permute-start.1) | collective-permute-done | bytes 657952 | tf_op jit(solution)/shard_map/ppermute | solution.py:40
  50.2 2.3 copy-done.6
  52.5 2.5 fusion.43
  55.0 2.2 copy.94
  57.3 4.6 %fusion.46 = bf16[4,257,320]{2,1,0:T(8,128)(2,1)} fusion(bf16[8,257,1280]{2,1,0:T(8,128)(2,1)} %copy-done.6, s32[]{:T(128)S(6)} %select_n.79, bf16[1280,320]{0,1:T(8,128)(2,1)} %param.11), kind=kOutput, calls=%fused_computation.45 | convolution fusion | flops 842466560 | bytes 4180484 | tf_op jit(solution)/shard_map/ctd,de->cte/dot_general | solution.py:52
  61.9 2.5 fusion.40
  64.4 2.3 copy.93
  66.7 2.3 copy.95
  69.0 6.5 %fusion.75 = (f32[4,4,257]{2,1,0:T(4,128)S(1)}, f32[4,4,257,257]{2,3,1,0:T(8,128)}) fusion(bf16[4,257,4,80]{1,3,2,0:T(8,128)(2,1)} %bitcast.109, bf16[4,257,4,80]{1,3,2,0:T(8,128)(2,1)} %bitcast.111), kind=kOutput, calls=%fused_computation.109 | convolution fusion | flops 172256048 | bytes 5559424 | tf_op jit(solution)/shard_map/sub | solution.py:64
  75.5 5.1 %fusion.39 = bf16[4,4,80,257]{3,2,1,0:T(8,128)(2,1)} fusion(bf16[4,257,4,80]{1,3,2,0:T(8,128)(2,1)} %bitcast.110, f32[4,4,257,257]{2,3,1,0:T(8,128)} %get-tuple-element.8, f32[4,4,257]{2,1,0:T(4,128)S(1)} %get-tuple-element.7), kind=kOutput, calls=%fused_computation.42 | convolution fusion | flops 171527968 | bytes 5559424 | tf_op jit(solution)/shard_map/chqk,ckhd->cqhd/dot_general | solution.py:65
  80.6 2.2 copy.97
  82.8 4.7 %all-to-all-start = ((bf16[4,257,320]{2,1,0:T(8,128)(2,1)}), bf16[4,257,320]{2,1,0:T(8,128)(2,1)}, u32[]{:S(2)}, u32[]{:S(2)}) async-start(bf16[4,257,320]{2,1,0:T(8,128)(2,1)} %copy.97), calls=%async_computation | async-start | bytes 1622016 | tf_op jit(solution)/shard_map/all_to_all | solution.py:71
  87.8 9.5 %all-to-all-done = bf16[4,257,320]{2,1,0:T(8,128)(2,1)} async-done(((bf16[4,257,320]{2,1,0:T(8,128)(2,1)}), bf16[4,257,320]{2,1,0:T(8,128)(2,1)}, u32[]{:S(2)}, u32[]{:S(2)}) %all-to-all-start) | async-done | bytes 657952 | tf_op jit(solution)/shard_map/all_to_all | solution.py:71
  97.3 2.3 copy.98
  99.6 2.5 reshape.358
  102.2 3.4 fusion.76
  107.7 6.4 %gather_fusion = bf16[768,1280]{1,0:T(8,128)(2,1)} fusion(bf16[257,1280]{1,0:T(8,128)(2,1)} %fusion.55, s32[1024]{0:T(1024)S(1)} %pad_clamp_fusion.1), kind=kCustom, calls=%fused_computation | custom fusion | bytes 3935232 | tf_op jit(solution)/shard_map/jit(_take)/gather | solution.py:88
  114.1 1.9 select_select_fusion
  116.5 101.9 %all_to_all.25 = bf16[128,1,24,1280]{3,2,1,0:T(8,128)(2,1)} all-to-all(bf16[128,1,24,1280]{3,2,1,0:T(8,128)(2,1)S(1)} %bitcast.107), channel_id=1, replica_groups=mesh['node'=4,'ep'=32] {'node','ep'}, dimensions={0} | all-to-all | bytes 15728640 | tf_op jit(solution)/shard_map/all_to_all | solution.py:93
  218.4 25.9 %convert_bitcast_fusion = bf16[128,1,24,1280]{3,0,2,1:T(8,128)(2,1)} fusion(bf16[1,1280,1280]{2,1,0:T(8,128)(2,1)S(1)} %copy-done, bf16[128,1,24,1280]{3,2,1,0:T(8,128)(2,1)} %all_to_all.25, bf16[1,1280,1280]{2,1,0:T(8,128)(2,1)} %param.15), kind=kOutput, calls=%fused_computation.18 | convolution fusion | flops 20171980800 | bytes 22282240 | tf_op jit(solution)/shard_map/lesf,efd->lesd/dot_general | solution.py:96
  244.3 10.8 %copy.108 = bf16[128,1,24,1280]{3,2,1,0:T(8,128)(2,1)} copy(bf16[128,1,24,1280]{3,0,2,1:T(8,128)(2,1)} %convert_bitcast_fusion) | data formatting | bytes 15728640 | tf_op jit(solution)/shard_map/convert_element_type | solution.py:98
  255.1 10.0 %all-to-all-start.2 = ((bf16[128,1,24,1280]{3,2,1,0:T(8,128)(2,1)}), bf16[128,1,24,1280]{3,2,1,0:T(8,128)(2,1)}, u32[]{:S(2)}, u32[]{:S(2)}) async-start(bf16[128,1,24,1280]{3,2,1,0:T(8,128)(2,1)} %copy.108), calls=%async_computation.2 | async-start | bytes 15728640 | tf_op jit(solution)/shard_map/all_to_all | solution.py:99
  266.1 98.2 %all-to-all-done.2 = bf16[128,1,24,1280]{3,2,1,0:T(8,128)(2,1)} async-done(((bf16[128,1,24,1280]{3,2,1,0:T(8,128)(2,1)}), bf16[128,1,24,1280]{3,2,1,0:T(8,128)(2,1)}, u32[]{:S(2)}, u32[]{:S(2)}) %all-to-all-start.2) | async-done | bytes 7864352 | tf_op jit(solution)/shard_map/all_to_all | solution.py:99
  364.3 4.3 %bitcast_reduce_fusion = bf16[32,24,1280]{2,1,0:T(8,128)(2,1)S(1)} fusion(bf16[4,32,24,1280]{3,2,1,0:T(8,128)(2,1)} %bitcast.104), kind=kLoop, calls=%fused_computation.13 | loop fusion | flops 2949120 | bytes 9830400 | tf_op jit(solution)/shard_map/reduce_sum | solution.py:103
  368.6 3.5 gather_fusion.1
  372.0 4.1 %gather.15 = bf16[1,257,2,1280]{3,2,1,0:T(2,128)(2,1)} reshape(bf16[514,1280]{1,0:T(8,128)(2,1)} %gather_fusion.1) | data formatting | bytes 2631680 | tf_op jit(solution)/shard_map/jit(_take)/gather | solution.py:105
  376.2 13.6 %multiply_reduce_fusion.1 = f32[257,1280]{1,0:T(8,128)S(1)} fusion(bf16[1,257,2,1280]{3,2,1,0:T(2,128)(2,1)} %gather.15, pred[257,2]{1,0:T(8,128)(4,1)S(1)} %copy.105, f32[257,2]{1,0:T(8,128)S(1)} %copy.99), kind=kLoop, calls=%fused_computation.29 | loop fusion | flops 2302720 | bytes 2634250 | tf_op jit(solution)/shard_map/reduce_sum | solution.py:106
  (76 shorter events, 19.7 us)
Async XLA Ops:
  0.0 218.4 %copy-start = (bf16[1,1280,1280]{2,1,0:T(8,128)(2,1)S(1)}, bf16[1,1280,1280]{2,1,0:T(8,128)(2,1)}, u32[]{:S(2)}) copy-start(bf16[1,1280,1280]{2,1,0:T(8,128)(2,1)} %param.16) | copy-start | bytes 9830404
  0.0 10.4 %copy-start.9 = (s32[1,257,2]{1,2,0:T(2,128)S(1)}, s32[1,257,2]{1,2,0:T(2,128)}, u32[]{:S(2)}) copy-start(s32[1,257,2]{1,2,0:T(2,128)} %param.17) | copy-start | bytes 6172
  5.2 40.0 %collective-permute-start.2 = (bf16[1,257,1280]{2,1,0:T(8,128)(2,1)}, bf16[1,257,1280]{2,1,0:T(8,128)(2,1)}, u32[]{:S(2)}, u32[]{:S(2)}) collective-permute-start(bf16[1,257,1280]{2,1,0:T(8,128)(2,1)} %fusion.50), channel_id=1, source_target_pairs={{0,96},{32,0},{64,32},{96,64},{1,97},{33,1},{65,33},{97,65},{2,98}... | collective-permute-start | bytes 1973768 | tf_op jit(solution)/shard_map/ppermute | solution.py:44
  7.6 17.3 %collective-permute-start = (bf16[1,257,1280]{2,1,0:T(8,128)(2,1)}, bf16[1,257,1280]{2,1,0:T(8,128)(2,1)}, u32[]{:S(2)}, u32[]{:S(2)}) collective-permute-start(bf16[1,257,1280]{2,1,0:T(8,128)(2,1)} %fusion.50), channel_id=1, source_target_pairs={{0,32},{32,64},{64,96},{96,0},{1,33},{33,65},{65,97},{97,1},{2,34}... | collective-permute-start | bytes 1973768 | tf_op jit(solution)/shard_map/ppermute | solution.py:40
  24.9 16.4 %collective-permute-start.1 = (bf16[1,257,1280]{2,1,0:T(8,128)(2,1)}, bf16[1,257,1280]{2,1,0:T(8,128)(2,1)}, u32[]{:S(2)}, u32[]{:S(2)}) collective-permute-start(bf16[1,257,1280]{2,1,0:T(8,128)(2,1)} %collective-permute-done), channel_id=1, source_target_pairs={{0,32},{32,64},{64,96},{96,0},{1,33},{33,65},{65,97},{97,1},{2,34}... | collective-permute-start | bytes 1973768 | tf_op jit(solution)/shard_map/ppermute | solution.py:40
  42.5 6.2 %copy-start.3 = (bf16[1,257,1280]{2,1,0:T(8,128)(2,1)S(1)}, bf16[1,257,1280]{2,1,0:T(8,128)(2,1)}, u32[]{:S(2)}) copy-start(bf16[1,257,1280]{2,1,0:T(8,128)(2,1)} %param.9) | copy-start | bytes 1973764
  45.2 7.3 %copy-start.10 = (bf16[1280,320]{0,1:T(8,128)(2,1)S(1)}, bf16[1280,320]{0,1:T(8,128)(2,1)}, u32[]{:S(2)}) copy-start(bf16[1280,320]{0,1:T(8,128)(2,1)} %param.10) | copy-start | bytes 2457604
  50.2 2.3 copy-start.6
  57.3 4.6 %copy-start.7 = (bf16[8,257,1280]{2,1,0:T(8,128)(2,1)S(1)}, bf16[8,257,1280]{2,1,0:T(8,128)(2,1)}, u32[]{:S(2)}) copy-start(bf16[8,257,1280]{2,1,0:T(8,128)(2,1)} %copy-done.6) | copy-start | bytes 15790084
  57.3 4.6 %copy-start.11 = (bf16[1280,320]{0,1:T(8,128)(2,1)S(1)}, bf16[1280,320]{0,1:T(8,128)(2,1)}, u32[]{:S(2)}) copy-start(bf16[1280,320]{0,1:T(8,128)(2,1)} %param.12) | copy-start | bytes 2457604
  82.8 14.5 %all-to-all-start = ((bf16[4,257,320]{2,1,0:T(8,128)(2,1)}), bf16[4,257,320]{2,1,0:T(8,128)(2,1)}, u32[]{:S(2)}, u32[]{:S(2)}) async-start(bf16[4,257,320]{2,1,0:T(8,128)(2,1)} %copy.97), calls=%async_computation | async-start | bytes 1622016 | tf_op jit(solution)/shard_map/all_to_all | solution.py:71
  105.6 1.1 copy-start.4
  255.1 10.5 %copy-start.2 = (bf16[257,1280]{1,0:T(8,128)(2,1)S(1)}, bf16[257,1280]{1,0:T(8,128)(2,1)}, u32[]{:S(2)}) copy-start(bf16[257,1280]{1,0:T(8,128)(2,1)} %fusion.55) | copy-start | bytes 1973764
  255.1 10.5 %copy-start.8 = (bf16[1280,32]{0,1:T(8,128)(2,1)S(1)}, bf16[1280,32]{0,1:T(8,128)(2,1)}, u32[]{:S(2)}) copy-start(bf16[1280,32]{0,1:T(8,128)(2,1)} %param.14) | copy-start | bytes 245764
  255.1 109.2 %all-to-all-start.2 = ((bf16[128,1,24,1280]{3,2,1,0:T(8,128)(2,1)}), bf16[128,1,24,1280]{3,2,1,0:T(8,128)(2,1)}, u32[]{:S(2)}, u32[]{:S(2)}) async-start(bf16[128,1,24,1280]{3,2,1,0:T(8,128)(2,1)} %copy.108), calls=%async_computation.2 | async-start | bytes 15728640 | tf_op jit(solution)/shard_map/all_to_all | solution.py:99
  372.0 18.7 %copy-start.1 = (bf16[1,1280,1280]{2,1,0:T(8,128)(2,1)S(1)}, bf16[1,1280,1280]{2,1,0:T(8,128)(2,1)}, u32[]{:S(2)}) copy-start(bf16[1,1280,1280]{2,1,0:T(8,128)(2,1)} %param.16) | copy-start | bytes 9830404
  376.2 13.6 %copy-start.5 = (f32[1,257,1280]{2,1,0:T(8,128)S(1)}, f32[1,257,1280]{2,1,0:T(8,128)}, u32[]{:S(2)}) copy-start(f32[1,257,1280]{2,1,0:T(8,128)} %copy-done.4) | copy-start | bytes 3947524
